TPU v7x, 32 devices: a whole 2x2x4 slice. The times are simulated.
32 devices in a mesh: groups: 2 (over y), tile: 4 (over z), chan: 2 (over x), low: 2 (over core).
Axes of the slice: x: 2, y: 2, z: 4, core: 2. Of those that a mesh axis runs over, the one named last changes fastest.
Arguments:
- latent_map: bfloat16 [16, 16, 16, 512], P('groups', 'tile', 'chan'), parts along dimension 0, may hold values from -6 to 6
- inner_map: bfloat16 [16, 16, 16, 512], P(('groups', 'tile'), None, 'chan'), parts along dimension 0, may hold values from -6 to 6
- timestep: int32 [16], P('groups'), parts along dimension 0, may hold values from 0 to 999
- conv_weight: bfloat16 [3, 3, 512, 512], P(None, None, None, 'low'), may hold values from -0.09375 to 0.09375
- time_weight: bfloat16 [256, 512], P(None, 'low'), may hold values from -0.375 to 0.375
- attend_weight: bfloat16 [3, 512, 512], P(None, None, 'low'), may hold values from -8 to 8
Outputs:
- attended: bfloat16 [16, 16, 16, 512], P(('groups', 'tile'), None, 'chan', 'low'), parts along dimension 0
There are 2 independent parts, one for each index of `groups`. A program takes and returns all parts, laid end to end along the dimension named above; an argument that names none is the same for every part. Nothing has to cross between parts.
All inputs are finite; a program needn't handle non-finite values.
Results may differ from a plain program's by a relative error of at most 0.017.
The roundings to bfloat16 on the way count: a program that leaves them out, or rounds other values in their place, can miss the bound.
Values may be sent and summed in bfloat16 or wider, within the bound.
No kernel may reach another device: no remote copies, remote signals or barrier semaphores. Data moves between devices by JAX's collectives and lax.ppermute only.
A program may use at most 64 MiB of HBM per device.

v0:
```python
import math
import jax
import jax.numpy as jnp
from jax import lax
from jax.sharding import PartitionSpec as P

HEAD = 64
TE = 256


def time_embedding(timestep):
    halfway = TE // 2
    ladder = jnp.arange(halfway, dtype=jnp.float32)
    frequency = jnp.exp(ladder * (-math.log(10000.0) / halfway))
    angles = timestep.astype(jnp.float32)[:, None] * frequency[None, :]
    return jnp.concatenate([jnp.sin(angles), jnp.cos(angles)], axis=1)


def swap(tree, axis):
    return lax.ppermute(tree, axis, [(0, 1), (1, 0)])


def convolve(joined, weight):
    return lax.conv_general_dilated(
        joined,
        weight,
        window_strides=(1, 1),
        padding=((1, 1), (1, 1)),
        dimension_numbers=("NHWC", "HWIO", "NHWC"),
        preferred_element_type=jnp.float32,
    )


def attend(queries, keys, values):
    scores = jnp.einsum("nqd,nkd->nqk", queries, keys, preferred_element_type=jnp.float32)
    scores = scores * HEAD ** (-0.5)
    row_peak = jnp.max(scores, axis=2, keepdims=True)
    weights = jnp.exp(scores - row_peak)
    totals = jnp.sum(weights, axis=2, keepdims=True)
    summed = jnp.einsum(
        "nqk,nkd->nqd", weights.astype(jnp.bfloat16), values, preferred_element_type=jnp.float32
    )
    return (summed / totals).astype(jnp.bfloat16)


def per_device(latent_map, inner_map, timestep, conv_weight, time_weight, attend_weight):
    tiles = lax.axis_size("tile")
    lows = lax.axis_size("low")
    t_idx = lax.axis_index("tile")
    c_idx = lax.axis_index("chan")
    l_idx = lax.axis_index("low")
    samples, row_local, col_local, width = latent_map.shape
    per_tile = samples // tiles
    per_core = per_tile // lows
    half = conv_weight.shape[3]
    heads_local = attend_weight.shape[2] // HEAD
    conv_other, time_other = swap((conv_weight, time_weight), "low")
    start = l_idx * per_core
    stamps = lax.dynamic_slice_in_dim(timestep, t_idx * per_tile + start, per_core, 0)
    embedded = time_embedding(stamps)
    mod_own = jnp.dot(embedded, time_weight.astype(jnp.float32), precision=lax.Precision.HIGHEST)
    mod_other = jnp.dot(embedded, time_other.astype(jnp.float32), precision=lax.Precision.HIGHEST)
    start = l_idx * per_core
    chans = lax.axis_size("chan")
    blocks = lax.dynamic_slice_in_dim(
        latent_map.reshape(tiles, per_tile, row_local, col_local, width), start, per_core, 1
    )
    inner_own = lax.dynamic_slice_in_dim(inner_map, start, per_core, 0)
    if tiles * chans <= 8 and chans == 2:
        outgoing = jnp.broadcast_to(blocks[:, None], (tiles, chans) + blocks.shape[1:])
        arrived = lax.all_to_all(
            outgoing.reshape((tiles * chans,) + blocks.shape[1:]),
            ("tile", "chan"),
            0,
            0,
            tiled=True,
        )
        arrived = arrived.reshape(tiles, chans, per_core, row_local, col_local, width)
        latent_whole = arrived.transpose(2, 0, 3, 1, 4, 5).reshape(
            per_core, tiles * row_local, chans * col_local, width
        )
        inner_gated, mod_own, mod_other = lax.optimization_barrier((inner_own, mod_own, mod_other))
        partner = swap(inner_gated, "chan")
        inner_whole = lax.dynamic_slice_in_dim(
            jnp.concatenate([inner_own, partner, inner_own], axis=2),
            c_idx * col_local,
            2 * col_local,
            2,
        )
        whole = (latent_whole.astype(jnp.float32) + inner_whole.astype(jnp.float32)).astype(
            jnp.bfloat16
        )
    else:
        outgoing = blocks.reshape(tiles * per_core, row_local, col_local, width)
        arrived = lax.all_to_all(outgoing, "tile", split_axis=0, concat_axis=1, tiled=True)
        joined = (arrived.astype(jnp.float32) + inner_own.astype(jnp.float32)).astype(jnp.bfloat16)
        whole = lax.all_gather(joined, "chan", axis=2, tiled=True)

    def features_of(weight, modulation):
        convolved = convolve(whole, weight)
        return jax.nn.silu(convolved * (1.0 + modulation[:, None, None, :])).astype(jnp.bfloat16)

    feat_own = features_of(conv_weight, mod_own)
    feat_other = features_of(conv_other, mod_other)
    nat_own = lax.dynamic_slice_in_dim(
        jnp.concatenate([feat_own, feat_other, feat_own], axis=3), l_idx * half, 2 * half, 3
    )
    nat_part = swap(nat_own, "low")
    features = lax.dynamic_slice_in_dim(
        jnp.concatenate([nat_own, nat_part, nat_own], axis=0), l_idx * per_core, per_tile, 0
    )
    rows_total, cols_total = (features.shape[1], features.shape[2])
    tokens = rows_total * cols_total

    def project(part, which):
        return jnp.dot(part, attend_weight[which], preferred_element_type=jnp.float32).astype(
            jnp.bfloat16
        )

    own_cols = lax.dynamic_slice_in_dim(features, c_idx * col_local, col_local, 2)
    flat = features.reshape(per_tile, tokens, width)
    queries = project(own_cols.reshape(per_tile, -1, width), 0)
    keys = project(flat, 1)
    values = project(flat, 2)
    query_count = queries.shape[1]
    if tokens * query_count * 4 * per_tile * heads_local <= 8 << 20:
        split = lambda x: x.reshape(per_tile, x.shape[1], heads_local, HEAD)
        q4, k4, v4 = (split(queries), split(keys), split(values))
        scores = jnp.einsum("bqhd,bkhd->bhqk", q4, k4, preferred_element_type=jnp.float32)
        scores = scores * HEAD ** (-0.5)
        row_peak = jnp.max(scores, axis=3, keepdims=True)
        weights = jnp.exp(scores - row_peak)
        totals = jnp.sum(weights, axis=3)
        summed = jnp.einsum(
            "bhqk,bkhd->bqhd", weights.astype(jnp.bfloat16), v4, preferred_element_type=jnp.float32
        )
        out = (summed / totals.transpose(0, 2, 1)[..., None]).astype(jnp.bfloat16)
        return out.reshape(per_tile, rows_total, col_local, heads_local * HEAD)

    def by_head(x):
        n, k, _ = x.shape
        return (
            x.reshape(n, k, heads_local, HEAD)
            .transpose(0, 2, 1, 3)
            .reshape(n * heads_local, k, HEAD)
        )

    q_heads, k_heads, v_heads = (by_head(queries), by_head(keys), by_head(values))
    out = lax.map(lambda trio: attend(*(x[None] for x in trio))[0], (q_heads, k_heads, v_heads))
    out = out.reshape(per_tile, heads_local, rows_total, col_local, HEAD)
    return out.transpose(0, 2, 3, 1, 4).reshape(per_tile, rows_total, col_local, heads_local * HEAD)


def solution(mesh):
    in_specs = (
        P("groups", "tile", "chan", None),
        P(("groups", "tile"), None, "chan", None),
        P("groups"),
        P(None, None, None, "low"),
        P(None, "low"),
        P(None, None, "low"),
    )
    out_specs = P(("groups", "tile"), None, "chan", "low")
    return jax.shard_map(
        per_device, mesh=mesh, in_specs=in_specs, out_specs=out_specs, check_vma=False
    )
```

profile of v0, /device:TPU:0, one launch (start us, length us, event | category | flops | bytes accessed | tf_op | source)
XLA Modules:
  0.0 27.8 jit_solution(7526167668879524129)
XLA Ops:
  0.0 0.0 copy-start
  0.0 0.0 copy-start.2
  0.0 0.5 %collective-permute-start.2 = (bf16[3,3,512,256]{3,2,1,0:T(8,128)(2,1)}, bf16[3,3,512,256]{3,2,1,0:T(8,128)(2,1)S(1)}, u32[]{:S(2)}, u32[]{:S(2)}) collective-permute-start(bf16[3,3,512,256]{3,2,1,0:T(8,128)(2,1)} %param.9), channel_id=1, source_target_pairs={{0,1},{1,0},{2,3},{3,2},{4,5},{5,4},{6,7},{7,6},{8,9},{9,8},{10,11... | collective-permute-start | bytes 7077896 | tf_op jit(solution)/shard_map/ppermute | solution.py:20
  0.5 0.1 collective-permute-start
  0.5 0.4 %copy-done = bf16[8,4,8,512]{3,2,1,0:T(8,128)(2,1)S(1)} copy-done((bf16[8,4,8,512]{3,2,1,0:T(8,128)(2,1)S(1)}, bf16[8,4,8,512]{3,2,1,0:T(8,128)(2,1)}, u32[]{:S(2)}) %copy-start) | copy-done | bytes 262168
  1.0 0.7 %broadcast_in_dim.7 = bf16[4,2,4,8,512]{4,3,2,1,0:T(8,128)(2,1)} broadcast(bf16[4,4,8,512]{3,2,1,0:T(8,128)(2,1)S(1)} %dynamic-slice_bitcast_fusion), dimensions={0,2,3,4} | broadcast | bytes 393216 | tf_op jit(solution)/shard_map/broadcast_in_dim | solution.py:70
  1.7 7.3 %all-to-all-start = ((bf16[8,1,4,8,512]{4,3,2,1,0:T(8,128)(2,1)}), bf16[8,1,4,8,512]{4,3,2,1,0:T(8,128)(2,1)S(1)}, u32[]{:S(2)}, u32[]{:S(2)}) async-start(bf16[8,1,4,8,512]{4,3,2,1,0:T(8,128)(2,1)} %bitcast.2), calls=%async_computation | async-start | bytes 524288 | tf_op jit(solution)/shard_map/all_to_all | solution.py:71
  8.9 1.2 %dynamic_slice.24 = s32[1]{0:T(128)} dynamic-slice(s32[8]{0:T(128)} %param.8, s32[]{:T(128)S(6)} %select_n.24), dynamic_slice_sizes={1} | dynamic-slice | bytes 12 | tf_op jit(solution)/shard_map/dynamic_slice | solution.py:59
  10.8 0.1 fusion.25
  10.9 1.0 %fusion.34 = f32[1,256]{1,0:T(1,128)S(1)} fusion(bf16[256,256]{1,0:T(8,128)(2,1)} %param.10, f32[1,128]{1,0:T(1,128)S(1)} %get-tuple-element.13, f32[1,128]{1,0:T(1,128)S(1)} %get-tuple-element.14), kind=kOutput, calls=%fused_computation.58 | convolution fusion | flops 786688 | bytes 133120 | tf_op jit(solution)/shard_map/dot_general | solution.py:61
  11.9 0.0 copy-done.2
  11.9 0.1 constant_dynamic-slice_fusion.2
  12.0 0.0 collective-permute-done
  12.0 0.1 fusion.33
  12.1 2.1 %collective-permute-start.1 = (bf16[1,16,8,512]{3,2,1,0:T(8,128)(2,1)S(1)}, bf16[1,16,8,512]{3,2,1,0:T(8,128)(2,1)S(1)}, u32[]{:S(2)}, u32[]{:S(2)}) collective-permute-start(bf16[1,16,8,512]{3,2,1,0:T(8,128)(2,1)S(1)} %constant_dynamic-slice_fusion.2), channel_id=1, source_target_pairs={{0,2},{2,0},{1,3},{3,1},{4,6},{6,4},{5,7},{7,5},{8,10},{10,8},{9,1... | collective-permute-start | bytes 393224 | tf_op jit(solution)/shard_map/ppermute | solution.py:20
  14.2 3.7 %all-to-all-done = bf16[8,1,4,8,512]{4,3,2,1,0:T(8,128)(2,1)S(1)} async-done(((bf16[8,1,4,8,512]{4,3,2,1,0:T(8,128)(2,1)}), bf16[8,1,4,8,512]{4,3,2,1,0:T(8,128)(2,1)S(1)}, u32[]{:S(2)}, u32[]{:S(2)}) %all-to-all-start) | async-done | bytes 262176 | tf_op jit(solution)/shard_map/all_to_all | solution.py:71
  18.1 0.1 collective-permute-done.1
  18.2 0.1 fusion.23
  18.3 0.0 copy-start.3
  18.4 0.0 copy-start.4
  18.4 0.2 copy.42
  18.6 0.2 copy.33
  18.8 0.1 slice.15
  18.9 1.2 %copy-done.3 = bf16[3,3,512,256]{3,2,1,0:T(8,128)(2,1)S(1)} copy-done((bf16[3,3,512,256]{3,2,1,0:T(8,128)(2,1)S(1)}, bf16[3,3,512,256]{3,2,1,0:T(8,128)(2,1)}, u32[]{:S(2)}) %copy-start.3) | copy-done | bytes 2359320
  20.0 0.0 copy-done.4
  20.0 1.1 %multiply_convert_fusion.1 = bf16[16,8,3,256]{3,1,2,0:T(8,128)(2,1)S(1)} fusion(bf16[3,3,512,256]{3,2,1,0:T(8,128)(2,1)S(1)} %copy-done.3, bf16[16,1,7,2,512]{4,2,3,0,1:T(8,128)(2,1)S(1)} %slice.15, bf16[16,1,8,3,512]{4,2,3,0,1:T(8,128)(2,1)S(1)} %copy.33, f32[256]{0:T(256)S(1)} %bitcast.84, pred[8,3]{0,1:T(4,128)(4,1)S(1)} %copy-done.4), kind=kOutput, calls=%fused_computation.27 | convolution fusion | flops 870875136 | bytes 3179544 | tf_op jit(solution)/shard_map/conv_general_dilated | solution.py:24
  21.1 0.0 collective-permute-done.2
  21.1 1.1 %multiply_convert_fusion = bf16[16,8,3,256]{3,1,2,0:T(8,128)(2,1)S(1)} fusion(bf16[3,3,512,256]{3,2,1,0:T(8,128)(2,1)S(1)} %collective-permute-done.2, bf16[16,1,7,2,512]{4,2,3,0,1:T(8,128)(2,1)S(1)} %slice.15, bf16[16,1,8,3,512]{4,2,3,0,1:T(8,128)(2,1)S(1)} %copy.33, f32[256]{0:T(256)S(1)} %bitcast.83, pred[8,3]{0,1:T(4,128)(4,1)S(1)} %copy-done.4), kind=kOutput, calls=%fused_computation.26 | convolution fusion | flops 870875136 | bytes 3179544 | tf_op jit(solution)/shard_map/conv_general_dilated | solution.py:24
  22.3 0.1 copy.34
  22.5 0.2 copy.44
  22.7 0.0 copy-start.1
  22.7 0.1 collective-permute-start.3
  22.8 1.5 %collective-permute-done.3 = bf16[1,16,16,512]{3,2,1,0:T(8,128)(2,1)S(1)} collective-permute-done((bf16[1,16,16,512]{3,2,1,0:T(8,128)(2,1)S(1)}, bf16[1,16,16,512]{3,2,1,0:T(8,128)(2,1)S(1)}, u32[]{:S(2)}, u32[]{:S(2)}) %collective-permute-start.3) | collective-permute-done | bytes 262176 | tf_op jit(solution)/shard_map/ppermute | solution.py:20
  24.3 0.1 pad_maximum_fusion
  24.4 0.0 copy-done.1
  24.4 0.3 %convolution_convert_fusion = bf16[2,256,256]{1,2,0:T(8,128)(2,1)S(1)} fusion(bf16[2,256,512]{2,1,0:T(8,128)(2,1)S(1)} %bitcast.71, bf16[3,512,256]{2,1,0:T(8,128)(2,1)S(1)} %copy-done.1), kind=kOutput, calls=%fused_computation.3 | convolution fusion | flops 134348800 | bytes 1048576 | tf_op jit(solution)/shard_map/dot_general | solution.py:116
  24.8 0.3 %convolution_convert_fusion.1 = bf16[2,256,256]{1,2,0:T(8,128)(2,1)S(1)} fusion(bf16[2,256,512]{2,1,0:T(8,128)(2,1)S(1)} %bitcast.72, bf16[3,512,256]{2,1,0:T(8,128)(2,1)S(1)} %copy-done.1), kind=kOutput, calls=%fused_computation.4 | convolution fusion | flops 134348800 | bytes 1048576 | tf_op jit(solution)/shard_map/dot_general | solution.py:116
  25.2 0.2 convolution_convert_fusion.2
  25.4 0.1 copy.37
  25.5 0.4 %fusion.35 = (f32[2,4,128]{2,1,0:T(4,128)S(1)}, f32[2,4,128,256]{3,2,1,0:T(8,128)S(1)}) fusion(bf16[2,128,4,64]{1,3,2,0:T(8,128)(2,1)S(1)} %bitcast.80, bf16[2,256,4,64]{1,3,2,0:T(8,128)(2,1)S(1)} %bitcast.79), kind=kOutput, calls=%fused_computation.59 | convolution fusion | flops 34077696 | bytes 1445888 | tf_op jit(solution)/shard_map/bqhd,bkhd->bhqk/dot_general | solution.py:129
  26.0 0.4 %fusion.5 = f32[2,4,128]{2,1,0:T(4,128)S(1)} fusion(f32[2,4,128,256]{3,2,1,0:T(8,128)S(1)} %get-tuple-element.12, f32[2,4,128]{2,1,0:T(4,128)S(1)} %get-tuple-element.11), kind=kLoop, calls=%fused_computation.14 | loop fusion | flops 523264 | bytes 1056768 | tf_op jit(solution)/shard_map/reduce_sum | solution.py:133
  26.3 0.4 %fusion.4 = bf16[2,128,4,64]{1,3,2,0:T(8,128)(2,1)S(1)} fusion(bf16[2,256,4,64]{1,3,2,0:T(8,128)(2,1)S(1)} %bitcast.81, f32[2,4,128,256]{3,2,1,0:T(8,128)S(1)} %get-tuple-element.12, f32[2,4,128]{2,1,0:T(4,128)S(1)} %get-tuple-element.11, f32[2,128,4]{1,2,0:T(4,128)S(1)} %bitcast.82), kind=kOutput, calls=%fused_computation.11 | convolution fusion | flops 34209792 | bytes 1449984 | tf_op jit(solution)/shard_map/bhqk,bkhd->bqhd/dot_general | solution.py:134
  26.7 0.2 copy.39
  26.9 0.9 %reshape.109 = bf16[2,16,8,256]{3,2,1,0:T(8,128)(2,1)} reshape(bf16[2,128,4,64]{3,2,1,0:T(4,128)(2,1)S(1)} %copy.39) | data formatting | bytes 262144 | tf_op jit(solution)/shard_map/reshape | solution.py:138
  (10 shorter events, 0.3 us)
Async XLA Ops:
  0.0 1.0 %copy-start = (bf16[8,4,8,512]{3,2,1,0:T(8,128)(2,1)S(1)}, bf16[8,4,8,512]{3,2,1,0:T(8,128)(2,1)}, u32[]{:S(2)}) copy-start(bf16[8,4,8,512]{3,2,1,0:T(8,128)(2,1)} %param.6) | copy-start | bytes 786436
  0.0 11.9 %copy-start.2 = (bf16[2,16,8,512]{3,2,1,0:T(8,128)(2,1)S(1)}, bf16[2,16,8,512]{3,2,1,0:T(8,128)(2,1)}, u32[]{:S(2)}) copy-start(bf16[2,16,8,512]{3,2,1,0:T(8,128)(2,1)} %param.7) | copy-start | bytes 786436
  0.0 21.1 %collective-permute-start.2 = (bf16[3,3,512,256]{3,2,1,0:T(8,128)(2,1)}, bf16[3,3,512,256]{3,2,1,0:T(8,128)(2,1)S(1)}, u32[]{:S(2)}, u32[]{:S(2)}) collective-permute-start(bf16[3,3,512,256]{3,2,1,0:T(8,128)(2,1)} %param.9), channel_id=1, source_target_pairs={{0,1},{1,0},{2,3},{3,2},{4,5},{5,4},{6,7},{7,6},{8,9},{9,8},{10,11... | collective-permute-start | bytes 7077896 | tf_op jit(solution)/shard_map/ppermute | solution.py:20
  0.5 11.5 %collective-permute-start = (bf16[256,256]{1,0:T(8,128)(2,1)}, bf16[256,256]{1,0:T(8,128)(2,1)S(1)}, u32[]{:S(2)}, u32[]{:S(2)}) collective-permute-start(bf16[256,256]{1,0:T(8,128)(2,1)} %param.10), channel_id=1, source_target_pairs={{0,1},{1,0},{2,3},{3,2},{4,5},{5,4},{6,7},{7,6},{8,9},{9,8},{10,11... | collective-permute-start | bytes 393224 | tf_op jit(solution)/shard_map/ppermute | solution.py:20
  1.7 16.3 %all-to-all-start = ((bf16[8,1,4,8,512]{4,3,2,1,0:T(8,128)(2,1)}), bf16[8,1,4,8,512]{4,3,2,1,0:T(8,128)(2,1)S(1)}, u32[]{:S(2)}, u32[]{:S(2)}) async-start(bf16[8,1,4,8,512]{4,3,2,1,0:T(8,128)(2,1)} %bitcast.2), calls=%async_computation | async-start | bytes 524288 | tf_op jit(solution)/shard_map/all_to_all | solution.py:71
  12.1 6.1 %collective-permute-start.1 = (bf16[1,16,8,512]{3,2,1,0:T(8,128)(2,1)S(1)}, bf16[1,16,8,512]{3,2,1,0:T(8,128)(2,1)S(1)}, u32[]{:S(2)}, u32[]{:S(2)}) collective-permute-start(bf16[1,16,8,512]{3,2,1,0:T(8,128)(2,1)S(1)} %constant_dynamic-slice_fusion.2), channel_id=1, source_target_pairs={{0,2},{2,0},{1,3},{3,1},{4,6},{6,4},{5,7},{7,5},{8,10},{10,8},{9,1... | collective-permute-start | bytes 393224 | tf_op jit(solution)/shard_map/ppermute | solution.py:20
  18.3 1.7 %copy-start.3 = (bf16[3,3,512,256]{3,2,1,0:T(8,128)(2,1)S(1)}, bf16[3,3,512,256]{3,2,1,0:T(8,128)(2,1)}, u32[]{:S(2)}) copy-start(bf16[3,3,512,256]{3,2,1,0:T(8,128)(2,1)} %param.9) | copy-start | bytes 7077892
  18.4 1.7 %copy-start.4 = (pred[8,3]{0,1:T(4,128)(4,1)S(1)}, pred[8,3]{0,1:T(4,128)(4,1)}, u32[]{:S(2)}) copy-start(pred[8,3]{0,1:T(4,128)(4,1)} %constant.69) | copy-start | bytes 76
  22.7 1.8 %copy-start.1 = (bf16[3,512,256]{2,1,0:T(8,128)(2,1)S(1)}, bf16[3,512,256]{2,1,0:T(8,128)(2,1)}, u32[]{:S(2)}) copy-start(bf16[3,512,256]{2,1,0:T(8,128)(2,1)} %param.11) | copy-start | bytes 2359300
  22.7 1.6 %collective-permute-start.3 = (bf16[1,16,16,512]{3,2,1,0:T(8,128)(2,1)S(1)}, bf16[1,16,16,512]{3,2,1,0:T(8,128)(2,1)S(1)}, u32[]{:S(2)}, u32[]{:S(2)}) collective-permute-start(bf16[1,16,16,512]{3,2,1,0:T(8,128)(2,1)S(1)} %bitcast.77), channel_id=1, source_target_pairs={{0,1},{1,0},{2,3},{3,2},{4,5},{5,4},{6,7},{7,6},{8,9},{9,8},{10,11... | collective-permute-start | bytes 786440 | tf_op jit(solution)/shard_map/ppermute | solution.py:20
where the time goes:
time: 28.1 us; the launch traced here: 27.8 us
  starting transfers between devices  9.92 us (35%)
  local copies, waits for them, and re-layouts  5.66 us (20%)
  waiting for transfers between devices  5.39 us (19%)
  matrix products  5.18 us (18%)
  between operations  0.89 us (3%)
  other arithmetic  0.77 us (3%)
    all_to_all x1, starting transfers between devices, per_device(): lax.all_to_all(outgoing.reshape((tiles * chans,) + blocks.shape[1:]), ('t...  7.25 us
    all_to_all x1, waiting for transfers between devices, per_device(): lax.all_to_all(outgoing.reshape((tiles * chans,) + blocks.shape[1:]), ('t...  3.75 us
    ppermute x4, starting transfers between devices, swap(): return lax.ppermute(tree, axis, [(0, 1), (1, 0)])  2.67 us
    conv_general_dilated x2, matrix products, convolve(): lax.conv_general_dilated(joined, weight, window_strides=(1, 1), padding=(...  2.25 us
    unnamed x11, local copies, waits for them, and re-layouts  1.74 us
    ppermute x4, waiting for transfers between devices, swap(): return lax.ppermute(tree, axis, [(0, 1), (1, 0)])  1.65 us
    dynamic_slice x1, local copies, waits for them, and re-layouts, per_device(): lax.dynamic_slice_in_dim(timestep, t_idx * per_tile + start, per_core, 0)  1.24 us
    dot_general x1, matrix products, per_device(): jnp.dot(embedded, time_weight.astype(jnp.float32), precision=lax.Precisio...  1.04 us
  transfers between devices with their start and end apart: 5, of which 3 were waited for; matrix products, arithmetic and copies ran while one was open for 18% of the time, Pallas kernels for 0%

commit v1 on v0

--- a/solution.py
+++ b/solution.py
@@ -68,13 +68,22 @@
     inner_own = lax.dynamic_slice_in_dim(inner_map, start, per_core, 0)
     if tiles * chans <= 8 and chans == 2:
         outgoing = jnp.broadcast_to(blocks[:, None], (tiles, chans) + blocks.shape[1:])
-        arrived = lax.all_to_all(
-            outgoing.reshape((tiles * chans,) + blocks.shape[1:]),
-            ("tile", "chan"),
-            0,
-            0,
-            tiled=True,
-        )
+        x_2 = outgoing.reshape((tiles * chans,) + blocks.shape[1:])
+        ways, here = (lax.axis_size(("tile", "chan")), lax.axis_index(("tile", "chan")))
+        width_2 = x_2.shape[0] // ways
+        shape = list(x_2.shape)
+        shape[0] = width_2
+        height = shape[0]
+        shape[0] = height * ways
+        full = jnp.zeros(shape, x_2.dtype)
+        for mask in range(ways):
+            part_2 = lax.dynamic_slice_in_dim(x_2, (here ^ mask) * width_2, width_2, axis=0)
+            if mask:
+                part_2 = lax.ppermute(
+                    part_2, ("tile", "chan"), [(d, d ^ mask) for d in range(ways)]
+                )
+            full = lax.dynamic_update_slice_in_dim(full, part_2, (here ^ mask) * height, axis=0)
+        arrived = full
         arrived = arrived.reshape(tiles, chans, per_core, row_local, col_local, width)
         latent_whole = arrived.transpose(2, 0, 3, 1, 4, 5).reshape(
             per_core, tiles * row_local, chans * col_local, width

time: 28.1 us -> 39.9 us (1.42)
  starting transfers between devices: 9.92 us -> 16.5 us
  waiting for transfers between devices: 5.39 us -> 9.9 us
  matrix products: 5.18 us -> 5.91 us
    ppermute x0 -> x7, starting transfers between devices: none -> 15.3 us  [per_device(): lax.ppermute(part_2, ('tile', 'chan'), [(d, d ^ mask) for d in range(ways)])]
    all_to_all x1 -> x0, starting transfers between devices: 7.25 us -> none  [per_device(): lax.all_to_all(outgoing.reshape((tiles * chans,) + blocks.shape[1:]), ('t...]
    ppermute x4, waiting for transfers between devices: 1.65 us -> 5.94 us  [swap(): return lax.ppermute(tree, axis, [(0, 1), (1, 0)])]
    ppermute x0 -> x7, waiting for transfers between devices: none -> 3.96 us  [per_device(): lax.ppermute(part_2, ('tile', 'chan'), [(d, d ^ mask) for d in range(ways)])]
    all_to_all x1 -> x0, waiting for transfers between devices: 3.75 us -> none  [per_device(): lax.all_to_all(outgoing.reshape((tiles * chans,) + blocks.shape[1:]), ('t...]
    conv_general_dilated x2, matrix products: 2.25 us -> 3.88 us  [convolve(): lax.conv_general_dilated(joined, weight, window_strides=(1, 1), padding=(...]
    ppermute x4, starting transfers between devices: 2.67 us -> 1.17 us  [swap(): return lax.ppermute(tree, axis, [(0, 1), (1, 0)])]
    dot_general x1, matrix products: 1.04 us -> 0.14 us  [per_device(): jnp.dot(embedded, time_weight.astype(jnp.float32), precision=lax.Precisio...]
  transfers between devices with their start and end apart: 5 -> 11, of which waited for: 3 -> 3; matrix products, arithmetic and copies ran while one was open for 18% -> 9% of each run, Pallas kernels for 0% -> 0%
where the time goes in v1:
time: 39.9 us; the launch traced here: 39.7 us
  starting transfers between devices  16.5 us (41%)
  waiting for transfers between devices  9.9 us (25%)
  matrix products  5.91 us (15%)
  local copies, waits for them, and re-layouts  5.67 us (14%)
  between operations  0.98 us (2%)
  other arithmetic  0.77 us (2%)
    ppermute x7, starting transfers between devices, per_device(): lax.ppermute(part_2, ('tile', 'chan'), [(d, d ^ mask) for d in range(ways)])  15.3 us
    ppermute x4, waiting for transfers between devices, swap(): return lax.ppermute(tree, axis, [(0, 1), (1, 0)])  5.94 us
    ppermute x7, waiting for transfers between devices, per_device(): lax.ppermute(part_2, ('tile', 'chan'), [(d, d ^ mask) for d in range(ways)])  3.96 us
    conv_general_dilated x2, matrix products, convolve(): lax.conv_general_dilated(joined, weight, window_strides=(1, 1), padding=(...  3.88 us
    unnamed x13, local copies, waits for them, and re-layouts  2.35 us
    dynamic_slice x1, local copies, waits for them, and re-layouts, per_device(): lax.dynamic_slice_in_dim(timestep, t_idx * per_tile + start, per_core, 0)  1.24 us
    ppermute x4, starting transfers between devices, swap(): return lax.ppermute(tree, axis, [(0, 1), (1, 0)])  1.17 us
    dot_general x3, matrix products, project(): jnp.dot(part, attend_weight[which], preferred_element_type=jnp.float32)  0.94 us
  transfers between devices with their start and end apart: 11, of which 3 were waited for; matrix products, arithmetic and copies ran while one was open for 9% of the time, Pallas kernels for 0%

profile of v1, /device:TPU:0, one launch (start us, length us, event | category | flops | bytes accessed | tf_op | source)
XLA Modules:
  0.0 39.7 jit_solution(4931467749781285617)
XLA Ops:
  0.0 0.0 copy-start
  0.0 0.0 copy-start.2
  0.0 0.0 copy-start.3
  0.0 1.0 %copy-done = bf16[8,4,8,512]{3,2,1,0:T(8,128)(2,1)S(1)} copy-done((bf16[8,4,8,512]{3,2,1,0:T(8,128)(2,1)S(1)}, bf16[8,4,8,512]{3,2,1,0:T(8,128)(2,1)}, u32[]{:S(2)}) %copy-start) | copy-done | bytes 262168
  1.1 3.0 %collective-permute-start = (bf16[1,1,4,8,512]{4,3,2,0,1:T(8,128)(2,1)S(1)}, bf16[1,1,4,8,512]{4,3,2,0,1:T(8,128)(2,1)S(1)}, u32[]{:S(2)}, u32[]{:S(2)}) collective-permute-start(bf16[1,1,4,8,512]{4,3,2,0,1:T(8,128)(2,1)S(1)} %get-tuple-element.17), channel_id=1, source_target_pairs={{0,2},{2,0},{4,6},{6,4},{8,10},{10,8},{12,14},{14,12},{1,3},{3,1},... | collective-permute-start | bytes 98312 | tf_op jit(solution)/shard_map/ppermute | solution.py:82
  4.1 1.6 %collective-permute-start.1 = (bf16[1,1,4,8,512]{4,3,2,0,1:T(8,128)(2,1)S(1)}, bf16[1,1,4,8,512]{4,3,2,0,1:T(8,128)(2,1)S(1)}, u32[]{:S(2)}, u32[]{:S(2)}) collective-permute-start(bf16[1,1,4,8,512]{4,3,2,0,1:T(8,128)(2,1)S(1)} %get-tuple-element.16), channel_id=1, source_target_pairs={{0,4},{2,6},{4,0},{6,2},{8,12},{10,14},{12,8},{14,10},{1,5},{3,7},... | collective-permute-start | bytes 98312 | tf_op jit(solution)/shard_map/ppermute | solution.py:82
  5.7 0.0 collective-permute-start.2
  5.7 0.0 collective-permute-start.7
  5.7 0.5 %collective-permute-start.9 = (bf16[3,3,512,256]{3,2,1,0:T(8,128)(2,1)}, bf16[3,3,512,256]{3,2,1,0:T(8,128)(2,1)}, u32[]{:S(2)}, u32[]{:S(2)}) collective-permute-start(bf16[3,3,512,256]{3,2,1,0:T(8,128)(2,1)} %param.9), channel_id=1, source_target_pairs={{0,1},{1,0},{2,3},{3,2},{4,5},{5,4},{6,7},{7,6},{8,9},{9,8},{10,11... | collective-permute-start | bytes 7077896 | tf_op jit(solution)/shard_map/ppermute | solution.py:20
  6.2 1.2 %dynamic_slice.56 = s32[1]{0:T(128)} dynamic-slice(s32[8]{0:T(128)} %param.8, s32[]{:T(128)S(6)} %select_n.64), dynamic_slice_sizes={1} | dynamic-slice | bytes 12 | tf_op jit(solution)/shard_map/dynamic_slice | solution.py:59
  8.1 0.1 fusion.25
  8.1 0.0 copy-done.3
  8.2 0.0 copy-done.2
  8.2 0.1 fusion.34
  8.3 0.1 broadcast_in_dim.10
  8.4 0.0 collective-permute-done
  8.4 3.1 %collective-permute-start.3 = (bf16[1,1,4,8,512]{4,3,2,0,1:T(8,128)(2,1)S(1)}, bf16[1,1,4,8,512]{4,3,2,0,1:T(8,128)(2,1)S(1)}, u32[]{:S(2)}, u32[]{:S(2)}) collective-permute-start(bf16[1,1,4,8,512]{4,3,2,0,1:T(8,128)(2,1)S(1)} %get-tuple-element.14), channel_id=1, source_target_pairs={{0,8},{2,10},{4,12},{6,14},{8,0},{10,2},{12,4},{14,6},{1,9},{3,11}... | collective-permute-start | bytes 98312 | tf_op jit(solution)/shard_map/ppermute | solution.py:82
  11.5 0.0 collective-permute-done.1
  11.5 1.3 %collective-permute-start.4 = (bf16[1,1,4,8,512]{4,3,2,0,1:T(8,128)(2,1)S(1)}, bf16[1,1,4,8,512]{4,3,2,0,1:T(8,128)(2,1)S(1)}, u32[]{:S(2)}, u32[]{:S(2)}) collective-permute-start(bf16[1,1,4,8,512]{4,3,2,0,1:T(8,128)(2,1)S(1)} %get-tuple-element.13), channel_id=1, source_target_pairs={{0,10},{2,8},{4,14},{6,12},{8,2},{10,0},{12,6},{14,4},{1,11},{3,9}... | collective-permute-start | bytes 98312 | tf_op jit(solution)/shard_map/ppermute | solution.py:82
  12.9 0.0 collective-permute-done.2
  12.9 3.7 %collective-permute-start.5 = (bf16[1,1,4,8,512]{4,3,2,0,1:T(8,128)(2,1)S(1)}, bf16[1,1,4,8,512]{4,3,2,0,1:T(8,128)(2,1)S(1)}, u32[]{:S(2)}, u32[]{:S(2)}) collective-permute-start(bf16[1,1,4,8,512]{4,3,2,0,1:T(8,128)(2,1)S(1)} %get-tuple-element.12), channel_id=1, source_target_pairs={{0,12},{2,14},{4,8},{6,10},{8,4},{10,6},{12,0},{14,2},{1,13},{3,15... | collective-permute-start | bytes 98312 | tf_op jit(solution)/shard_map/ppermute | solution.py:82
  16.5 0.0 collective-permute-done.3
  16.5 2.7 %collective-permute-start.6 = (bf16[1,1,4,8,512]{4,3,2,0,1:T(8,128)(2,1)S(1)}, bf16[1,1,4,8,512]{4,3,2,0,1:T(8,128)(2,1)S(1)}, u32[]{:S(2)}, u32[]{:S(2)}) collective-permute-start(bf16[1,1,4,8,512]{4,3,2,0,1:T(8,128)(2,1)S(1)} %get-tuple-element.11), channel_id=1, source_target_pairs={{0,14},{2,12},{4,10},{6,8},{8,6},{10,4},{12,2},{14,0},{1,15},{3,13... | collective-permute-start | bytes 98312 | tf_op jit(solution)/shard_map/ppermute | solution.py:82
  19.2 0.0 collective-permute-done.4
  19.2 0.0 collective-permute-done.5
  19.3 3.9 %collective-permute-done.6 = bf16[1,1,4,8,512]{4,3,2,0,1:T(8,128)(2,1)S(1)} collective-permute-done((bf16[1,1,4,8,512]{4,3,2,0,1:T(8,128)(2,1)S(1)}, bf16[1,1,4,8,512]{4,3,2,0,1:T(8,128)(2,1)S(1)}, u32[]{:S(2)}, u32[]{:S(2)}) %collective-permute-start.6) | collective-permute-done | bytes 32800 | tf_op jit(solution)/shard_map/ppermute | solution.py:82
  23.3 0.0 collective-permute-done.7
  23.3 0.1 fusion.33
  23.5 0.6 %collective-permute-start.8 = (bf16[1,16,8,512]{3,2,1,0:T(8,128)(2,1)S(1)}, bf16[1,16,8,512]{3,2,1,0:T(8,128)(2,1)S(1)}, u32[]{:S(2)}, u32[]{:S(2)}) collective-permute-start(bf16[1,16,8,512]{3,2,1,0:T(8,128)(2,1)S(1)} %constant_dynamic-slice_fusion.2), channel_id=1, source_target_pairs={{0,2},{2,0},{1,3},{3,1},{4,6},{6,4},{5,7},{7,5},{8,10},{10,8},{9,1... | collective-permute-start | bytes 393224 | tf_op jit(solution)/shard_map/ppermute | solution.py:20
  24.0 4.4 %collective-permute-done.8 = bf16[1,16,8,512]{3,2,1,0:T(8,128)(2,1)S(1)} collective-permute-done((bf16[1,16,8,512]{3,2,1,0:T(8,128)(2,1)S(1)}, bf16[1,16,8,512]{3,2,1,0:T(8,128)(2,1)S(1)}, u32[]{:S(2)}, u32[]{:S(2)}) %collective-permute-start.8) | collective-permute-done | bytes 131104 | tf_op jit(solution)/shard_map/ppermute | solution.py:20
  28.5 0.1 fusion.23
  28.6 0.0 copy-start.4
  28.6 0.0 copy-start.5
  28.6 0.2 copy.31
  28.8 0.2 copy.22
  29.1 0.1 slice.15
  29.1 1.2 %copy-done.4 = bf16[3,3,512,256]{3,2,1,0:T(8,128)(2,1)S(1)} copy-done((bf16[3,3,512,256]{3,2,1,0:T(8,128)(2,1)S(1)}, bf16[3,3,512,256]{3,2,1,0:T(8,128)(2,1)}, u32[]{:S(2)}) %copy-start.4) | copy-done | bytes 2359320
  30.3 0.0 copy-done.5
  30.3 1.1 %multiply_convert_fusion.1 = bf16[16,8,3,256]{3,1,2,0:T(8,128)(2,1)S(1)} fusion(bf16[3,3,512,256]{3,2,1,0:T(8,128)(2,1)S(1)} %copy-done.4, bf16[16,1,7,2,512]{4,2,3,0,1:T(8,128)(2,1)S(1)} %slice.15, bf16[16,1,8,3,512]{4,2,3,0,1:T(8,128)(2,1)S(1)} %copy.22, f32[256]{0:T(256)S(1)} %bitcast.87, pred[8,3]{0,1:T(4,128)(4,1)S(1)} %copy-done.5), kind=kOutput, calls=%fused_computation.27 | convolution fusion | flops 870875136 | bytes 3179544 | tf_op jit(solution)/shard_map/conv_general_dilated | solution.py:24
  31.4 0.0 collective-permute-done.9
  31.4 2.8 %multiply_convert_fusion = bf16[16,8,3,256]{3,1,2,0:T(8,128)(2,1)S(1)} fusion(bf16[3,3,512,256]{3,2,1,0:T(8,128)(2,1)} %collective-permute-done.9, bf16[16,1,7,2,512]{4,2,3,0,1:T(8,128)(2,1)S(1)} %slice.15, bf16[16,1,8,3,512]{4,2,3,0,1:T(8,128)(2,1)S(1)} %copy.22, f32[256]{0:T(256)S(1)} %bitcast.86, pred[8,3]{0,1:T(4,128)(4,1)S(1)} %copy-done.5), kind=kOutput, calls=%fused_computation.26 | convolution fusion | flops 870875136 | bytes 3179544 | tf_op jit(solution)/shard_map/conv_general_dilated | solution.py:24
  34.2 0.1 copy.23
  34.4 0.2 copy.33
  34.6 0.0 copy-start.1
  34.6 0.1 collective-permute-start.10
  34.7 1.5 %collective-permute-done.10 = bf16[1,16,16,512]{3,2,1,0:T(8,128)(2,1)S(1)} collective-permute-done((bf16[1,16,16,512]{3,2,1,0:T(8,128)(2,1)S(1)}, bf16[1,16,16,512]{3,2,1,0:T(8,128)(2,1)S(1)}, u32[]{:S(2)}, u32[]{:S(2)}) %collective-permute-start.10) | collective-permute-done | bytes 262176 | tf_op jit(solution)/shard_map/ppermute | solution.py:20
  36.2 0.1 pad_maximum_fusion
  36.3 0.0 copy-done.1
  36.3 0.3 convolution_convert_fusion
  36.7 0.3 convolution_convert_fusion.1
  37.1 0.2 convolution_convert_fusion.2
  37.3 0.1 copy.26
  37.4 0.4 %fusion.35 = (f32[2,4,128]{2,1,0:T(4,128)S(1)}, f32[2,4,128,256]{3,2,1,0:T(8,128)S(1)}) fusion(bf16[2,128,4,64]{1,3,2,0:T(8,128)(2,1)S(1)} %bitcast.83, bf16[2,256,4,64]{1,3,2,0:T(8,128)(2,1)S(1)} %bitcast.82), kind=kOutput, calls=%fused_computation.74 | convolution fusion | flops 34077696 | bytes 1445888 | tf_op jit(solution)/shard_map/bqhd,bkhd->bhqk/dot_general | solution.py:138
  37.9 0.4 fusion.5
  38.3 0.4 fusion.4
  38.6 0.2 copy.28
  38.8 0.9 %reshape.110 = bf16[2,16,8,256]{3,2,1,0:T(8,128)(2,1)} reshape(bf16[2,128,4,64]{3,2,1,0:T(4,128)(2,1)S(1)} %copy.28) | data formatting | bytes 262144 | tf_op jit(solution)/shard_map/reshape | solution.py:147
  (21 shorter events, 0.4 us)
Async XLA Ops:
  0.0 1.0 %copy-start = (bf16[8,4,8,512]{3,2,1,0:T(8,128)(2,1)S(1)}, bf16[8,4,8,512]{3,2,1,0:T(8,128)(2,1)}, u32[]{:S(2)}) copy-start(bf16[8,4,8,512]{3,2,1,0:T(8,128)(2,1)} %param.6) | copy-start | bytes 786436
  0.0 8.2 %copy-start.2 = (bf16[256,256]{1,0:T(8,128)(2,1)S(1)}, bf16[256,256]{1,0:T(8,128)(2,1)}, u32[]{:S(2)}) copy-start(bf16[256,256]{1,0:T(8,128)(2,1)} %param.10) | copy-start | bytes 393220
  0.0 8.1 %copy-start.3 = (bf16[2,16,8,512]{3,2,1,0:T(8,128)(2,1)S(1)}, bf16[2,16,8,512]{3,2,1,0:T(8,128)(2,1)}, u32[]{:S(2)}) copy-start(bf16[2,16,8,512]{3,2,1,0:T(8,128)(2,1)} %param.7) | copy-start | bytes 786436
  1.1 7.3 %collective-permute-start = (bf16[1,1,4,8,512]{4,3,2,0,1:T(8,128)(2,1)S(1)}, bf16[1,1,4,8,512]{4,3,2,0,1:T(8,128)(2,1)S(1)}, u32[]{:S(2)}, u32[]{:S(2)}) collective-permute-start(bf16[1,1,4,8,512]{4,3,2,0,1:T(8,128)(2,1)S(1)} %get-tuple-element.17), channel_id=1, source_target_pairs={{0,2},{2,0},{4,6},{6,4},{8,10},{10,8},{12,14},{14,12},{1,3},{3,1},... | collective-permute-start | bytes 98312 | tf_op jit(solution)/shard_map/ppermute | solution.py:82
  4.1 7.4 %collective-permute-start.1 = (bf16[1,1,4,8,512]{4,3,2,0,1:T(8,128)(2,1)S(1)}, bf16[1,1,4,8,512]{4,3,2,0,1:T(8,128)(2,1)S(1)}, u32[]{:S(2)}, u32[]{:S(2)}) collective-permute-start(bf16[1,1,4,8,512]{4,3,2,0,1:T(8,128)(2,1)S(1)} %get-tuple-element.16), channel_id=1, source_target_pairs={{0,4},{2,6},{4,0},{6,2},{8,12},{10,14},{12,8},{14,10},{1,5},{3,7},... | collective-permute-start | bytes 98312 | tf_op jit(solution)/shard_map/ppermute | solution.py:82
  5.7 7.2 %collective-permute-start.2 = (bf16[1,1,4,8,512]{4,3,2,0,1:T(8,128)(2,1)S(1)}, bf16[1,1,4,8,512]{4,3,2,0,1:T(8,128)(2,1)S(1)}, u32[]{:S(2)}, u32[]{:S(2)}) collective-permute-start(bf16[1,1,4,8,512]{4,3,2,0,1:T(8,128)(2,1)S(1)} %get-tuple-element.15), channel_id=1, source_target_pairs={{0,6},{2,4},{4,2},{6,0},{8,14},{10,12},{12,10},{14,8},{1,7},{3,5},... | collective-permute-start | bytes 98312 | tf_op jit(solution)/shard_map/ppermute | solution.py:82
  5.7 17.6 %collective-permute-start.7 = (bf16[256,256]{1,0:T(8,128)(2,1)}, bf16[256,256]{1,0:T(8,128)(2,1)S(1)}, u32[]{:S(2)}, u32[]{:S(2)}) collective-permute-start(bf16[256,256]{1,0:T(8,128)(2,1)} %param.10), channel_id=1, source_target_pairs={{0,1},{1,0},{2,3},{3,2},{4,5},{5,4},{6,7},{7,6},{8,9},{9,8},{10,11... | collective-permute-start | bytes 393224 | tf_op jit(solution)/shard_map/ppermute | solution.py:20
  5.7 25.7 %collective-permute-start.9 = (bf16[3,3,512,256]{3,2,1,0:T(8,128)(2,1)}, bf16[3,3,512,256]{3,2,1,0:T(8,128)(2,1)}, u32[]{:S(2)}, u32[]{:S(2)}) collective-permute-start(bf16[3,3,512,256]{3,2,1,0:T(8,128)(2,1)} %param.9), channel_id=1, source_target_pairs={{0,1},{1,0},{2,3},{3,2},{4,5},{5,4},{6,7},{7,6},{8,9},{9,8},{10,11... | collective-permute-start | bytes 7077896 | tf_op jit(solution)/shard_map/ppermute | solution.py:20
  8.4 8.1 %collective-permute-start.3 = (bf16[1,1,4,8,512]{4,3,2,0,1:T(8,128)(2,1)S(1)}, bf16[1,1,4,8,512]{4,3,2,0,1:T(8,128)(2,1)S(1)}, u32[]{:S(2)}, u32[]{:S(2)}) collective-permute-start(bf16[1,1,4,8,512]{4,3,2,0,1:T(8,128)(2,1)S(1)} %get-tuple-element.14), channel_id=1, source_target_pairs={{0,8},{2,10},{4,12},{6,14},{8,0},{10,2},{12,4},{14,6},{1,9},{3,11}... | collective-permute-start | bytes 98312 | tf_op jit(solution)/shard_map/ppermute | solution.py:82
  11.5 7.7 %collective-permute-start.4 = (bf16[1,1,4,8,512]{4,3,2,0,1:T(8,128)(2,1)S(1)}, bf16[1,1,4,8,512]{4,3,2,0,1:T(8,128)(2,1)S(1)}, u32[]{:S(2)}, u32[]{:S(2)}) collective-permute-start(bf16[1,1,4,8,512]{4,3,2,0,1:T(8,128)(2,1)S(1)} %get-tuple-element.13), channel_id=1, source_target_pairs={{0,10},{2,8},{4,14},{6,12},{8,2},{10,0},{12,6},{14,4},{1,11},{3,9}... | collective-permute-start | bytes 98312 | tf_op jit(solution)/shard_map/ppermute | solution.py:82
  12.9 6.4 %collective-permute-start.5 = (bf16[1,1,4,8,512]{4,3,2,0,1:T(8,128)(2,1)S(1)}, bf16[1,1,4,8,512]{4,3,2,0,1:T(8,128)(2,1)S(1)}, u32[]{:S(2)}, u32[]{:S(2)}) collective-permute-start(bf16[1,1,4,8,512]{4,3,2,0,1:T(8,128)(2,1)S(1)} %get-tuple-element.12), channel_id=1, source_target_pairs={{0,12},{2,14},{4,8},{6,10},{8,4},{10,6},{12,0},{14,2},{1,13},{3,15... | collective-permute-start | bytes 98312 | tf_op jit(solution)/shard_map/ppermute | solution.py:82
  16.5 6.7 %collective-permute-start.6 = (bf16[1,1,4,8,512]{4,3,2,0,1:T(8,128)(2,1)S(1)}, bf16[1,1,4,8,512]{4,3,2,0,1:T(8,128)(2,1)S(1)}, u32[]{:S(2)}, u32[]{:S(2)}) collective-permute-start(bf16[1,1,4,8,512]{4,3,2,0,1:T(8,128)(2,1)S(1)} %get-tuple-element.11), channel_id=1, source_target_pairs={{0,14},{2,12},{4,10},{6,8},{8,6},{10,4},{12,2},{14,0},{1,15},{3,13... | collective-permute-start | bytes 98312 | tf_op jit(solution)/shard_map/ppermute | solution.py:82
  23.5 5.0 %collective-permute-start.8 = (bf16[1,16,8,512]{3,2,1,0:T(8,128)(2,1)S(1)}, bf16[1,16,8,512]{3,2,1,0:T(8,128)(2,1)S(1)}, u32[]{:S(2)}, u32[]{:S(2)}) collective-permute-start(bf16[1,16,8,512]{3,2,1,0:T(8,128)(2,1)S(1)} %constant_dynamic-slice_fusion.2), channel_id=1, source_target_pairs={{0,2},{2,0},{1,3},{3,1},{4,6},{6,4},{5,7},{7,5},{8,10},{10,8},{9,1... | collective-permute-start | bytes 393224 | tf_op jit(solution)/shard_map/ppermute | solution.py:20
  28.6 1.7 %copy-start.4 = (bf16[3,3,512,256]{3,2,1,0:T(8,128)(2,1)S(1)}, bf16[3,3,512,256]{3,2,1,0:T(8,128)(2,1)}, u32[]{:S(2)}) copy-start(bf16[3,3,512,256]{3,2,1,0:T(8,128)(2,1)} %param.9) | copy-start | bytes 7077892
  28.6 1.7 %copy-start.5 = (pred[8,3]{0,1:T(4,128)(4,1)S(1)}, pred[8,3]{0,1:T(4,128)(4,1)}, u32[]{:S(2)}) copy-start(pred[8,3]{0,1:T(4,128)(4,1)} %constant.80) | copy-start | bytes 76
  34.6 1.8 %copy-start.1 = (bf16[3,512,256]{2,1,0:T(8,128)(2,1)S(1)}, bf16[3,512,256]{2,1,0:T(8,128)(2,1)}, u32[]{:S(2)}) copy-start(bf16[3,512,256]{2,1,0:T(8,128)(2,1)} %param.11) | copy-start | bytes 2359300
  34.6 1.6 %collective-permute-start.10 = (bf16[1,16,16,512]{3,2,1,0:T(8,128)(2,1)S(1)}, bf16[1,16,16,512]{3,2,1,0:T(8,128)(2,1)S(1)}, u32[]{:S(2)}, u32[]{:S(2)}) collective-permute-start(bf16[1,16,16,512]{3,2,1,0:T(8,128)(2,1)S(1)} %bitcast.77), channel_id=1, source_target_pairs={{0,1},{1,0},{2,3},{3,2},{4,5},{5,4},{6,7},{7,6},{8,9},{9,8},{10,11... | collective-permute-start | bytes 786440 | tf_op jit(solution)/shard_map/ppermute | solution.py:20
